TPU v7x, 32 devices: a whole 2x2x4 slice. The times are simulated.
32 devices in a mesh: groups: 2 (over y), seq: 4 (over z), tensor: 4 (over x, core).
Axes of the slice: x: 2, y: 2, z: 4, core: 2. Of those that a mesh axis runs over, the one named last changes fastest.
Arguments:
- x_in: bfloat16 [4096, 5120], P(('groups', 'seq'), 'tensor'), parts along dimension 0, may hold values from -6 to 6
- z_gate: bfloat16 [4096, 5120], P(('groups', 'seq'), 'tensor'), parts along dimension 0, may hold values from -32 to 32
- bc_in: bfloat16 [4096, 256], P(('groups', 'seq')), parts along dimension 0, may hold values from -6 to 6
- step_size: float32 [80, 4096], P('tensor', ('groups', 'seq')), parts along dimension 1, may hold values from 0 to 0.4
- log_keep: float32 [80, 4096], P('tensor', ('groups', 'seq')), parts along dimension 1, may hold values from -1 to 0
- skip_gain: float32 [80], P('tensor'), may hold values from 0.5 to 2
- conv_x: bfloat16 [4, 5120], P(None, 'tensor'), may hold values from -3 to 3
- conv_bc: bfloat16 [4, 256], replicated, may hold values from -3 to 3
- norm_gain: float32 [5120], P('tensor'), may hold values from 0.1 to 1.9
- seg_ends: int32 [1024], P(('groups', 'seq')), parts along dimension 0, may hold values from 0 to 2047, as said below
- pool_query: bfloat16 [320, 5120], P(('groups', 'seq'), 'tensor'), parts along dimension 0, may hold values from -64 to 64
- pool_start: int32 [320], P(('groups', 'seq')), parts along dimension 0, may hold values from 0 to 255, as said below
- pool_stop: int32 [320], P(('groups', 'seq')), parts along dimension 0, may hold values from 64 to 512
Outputs:
- mixed_seq: bfloat16 [4096, 5120], P(('groups', 'seq'), 'tensor'), parts along dimension 0
- pooled: float32 [320, 5120], P(('groups', 'seq'), 'tensor'), parts along dimension 0
There are 2 independent parts, one for each index of `groups`. A program takes and returns all parts, laid end to end along the dimension named above; an argument that names none is the same for every part. Nothing has to cross between parts.
Inputs may be any that keep to these rules, and one draw needn't show every extreme that they name: The tokens fall into blocks of 512; block b holds exactly the 128 segment ends seg_ends[b * 128] to seg_ends[(b + 1) * 128 - 1], strictly increasing. pool_start < pool_stop for every pooled row.
All inputs are finite; a program needn't handle non-finite values.
Results may differ from a plain program's by a relative error of at most 0.039.
Values may be sent and summed in bfloat16 or wider, within the bound.
No kernel may reach another device: no remote copies, remote signals or barrier semaphores. Data moves between devices by JAX's collectives and lax.ppermute only.
A program may use at most 64 MiB of HBM per device.

v0:
```python
import math
import jax
import jax.numpy as jnp
from jax import lax
from jax.sharding import PartitionSpec as P

STRETCH = 256
POOL_HEADS = 32
EPSILON = 1e-05
MASKED = -1e30


def passed_along(value, axis, steps):
    count = lax.axis_size(axis)
    leading, last = (max(0, -steps), min(count, count - steps))
    return lax.ppermute(value, axis, [(source, source + steps) for source in range(leading, last)])


def prefix(part, axis, combine, identity):
    place = lax.axis_index(axis)
    gathered = jax.tree.map(lambda a: lax.all_gather(a, axis), part)
    state = jax.tree.map(lambda a, e: jnp.zeros_like(a) + jnp.asarray(e, a.dtype), part, identity)

    def one(lap, state):
        return combine(
            state, jax.tree.map(lambda a: lax.dynamic_index_in_dim(a, lap, 0, False), gathered)
        )

    return lax.fori_loop(0, place, one, state)


def silu_act(values):
    return values / (1.0 + jnp.exp(-values))


def causal_conv(before, current, weights):
    kernel_width = weights.shape[0]
    length = current.shape[0]
    padded = jnp.concatenate([before, current], axis=0)
    summed = jnp.zeros(current.shape, jnp.float32)
    for offset in range(kernel_width):
        summed = summed + padded[offset : offset + length].astype(jnp.float32) * weights[
            offset
        ].astype(jnp.float32)
    return silu_act(summed).astype(jnp.bfloat16)


def stretch_local(x_block, b_block, c_block, step_block, keep_block):
    block_len = x_block.shape[0]
    cumul_keep = jnp.cumsum(keep_block, axis=1)
    lower_mask = lax.broadcasted_iota(jnp.int32, (block_len, block_len), 0) >= lax.broadcasted_iota(
        jnp.int32, (block_len, block_len), 1
    )
    inner_prod = jnp.einsum("is,js->ij", c_block, b_block, preferred_element_type=jnp.float32)
    spread = cumul_keep[:, :, None] - cumul_keep[:, None, :]
    decay_mask = jnp.where(lower_mask[None], jnp.exp(jnp.where(lower_mask[None], spread, 0.0)), 0.0)
    mixing = (decay_mask * inner_prod[None] * step_block[:, None, :]).astype(jnp.bfloat16)
    intra_part = jnp.einsum("hij,jhp->ihp", mixing, x_block, preferred_element_type=jnp.float32)
    tail_weight = jnp.exp(cumul_keep[:, -1:] - cumul_keep) * step_block
    weighted = (tail_weight.T[:, :, None] * x_block.astype(jnp.float32)).astype(jnp.bfloat16)
    stretch_state = jnp.einsum("jhp,js->hps", weighted, b_block, preferred_element_type=jnp.float32)
    return (intra_part, stretch_state, cumul_keep)


def combine(earlier, later):
    return (earlier[0] * jnp.exp(later[1])[:, None, None] + later[0], earlier[1] + later[1])


def read_state(c_block, state_in):
    state_high = state_in.astype(jnp.bfloat16)
    state_low = (state_in - state_high.astype(jnp.float32)).astype(jnp.bfloat16)
    high_part = jnp.einsum("is,hps->ihp", c_block, state_high, preferred_element_type=jnp.float32)
    low_part = jnp.einsum("is,hps->ihp", c_block, state_low, preferred_element_type=jnp.float32)
    return high_part + low_part


def local(
    x_in,
    z_gate,
    bc_in,
    step_size,
    log_keep,
    skip_gain,
    conv_x,
    conv_bc,
    norm_gain,
    seg_ends,
    pool_query,
    pool_start,
    pool_stop,
):
    tok_rows = x_in.shape[0]
    channels = x_in.shape[1]
    heads_local = step_size.shape[0]
    head_width = channels // heads_local
    state_width = bc_in.shape[1] // 2
    rim_rows = conv_x.shape[0] - 1
    edge_rows = jnp.concatenate([x_in[tok_rows - rim_rows :], bc_in[tok_rows - rim_rows :]], axis=1)
    before = passed_along(edge_rows, "seq", 1)
    x_conv = causal_conv(before[:, :channels], x_in, conv_x)
    bc_conv = causal_conv(before[:, channels:], bc_in, conv_bc)
    b_mat = bc_conv[:, :state_width]
    c_mat = bc_conv[:, state_width:]
    x_heads = x_conv.reshape(tok_rows, heads_local, head_width)
    stretch_count = tok_rows // STRETCH
    entry_state = jnp.zeros((heads_local, head_width, state_width), jnp.float32)
    decay_total = jnp.zeros((heads_local,), jnp.float32)
    saved_parts = []
    for block_index in range(stretch_count):
        first_row = block_index * STRETCH
        last_row = first_row + STRETCH
        intra_part, stretch_state, cumul_keep = stretch_local(
            x_heads[first_row:last_row],
            b_mat[first_row:last_row],
            c_mat[first_row:last_row],
            step_size[:, first_row:last_row],
            log_keep[:, first_row:last_row],
        )
        saved_parts.append((intra_part, cumul_keep, entry_state, decay_total))
        entry_state = jnp.exp(cumul_keep[:, -1])[:, None, None] * entry_state + stretch_state
        decay_total = decay_total + cumul_keep[:, -1]
    incoming, unused = prefix(
        (entry_state, decay_total),
        "seq",
        combine,
        (jnp.zeros_like(entry_state), jnp.zeros_like(decay_total)),
    )
    pieces_out = []
    for block_index in range(stretch_count):
        intra_part, cumul_keep, entry_part, decay_part = saved_parts[block_index]
        first_row = block_index * STRETCH
        state_in = entry_part + jnp.exp(decay_part)[:, None, None] * incoming
        from_state = read_state(c_mat[first_row : first_row + STRETCH], state_in)
        pieces_out.append(intra_part + jnp.exp(cumul_keep).T[:, :, None] * from_state)
    ssd_out = jnp.concatenate(pieces_out, axis=0) + skip_gain[None, :, None] * x_heads.astype(
        jnp.float32
    )
    gated = ssd_out.reshape(tok_rows, channels) * silu_act(z_gate.astype(jnp.float32))
    square_sum = lax.psum(jnp.sum(gated * gated, axis=1), "tensor")
    width_all = channels * lax.axis_size("tensor")
    mixed_seq = (
        gated * lax.rsqrt(square_sum / width_all + EPSILON)[:, None] * norm_gain[None, :]
    ).astype(jnp.bfloat16)
    local_ends = seg_ends - lax.axis_index("seq") * tok_rows
    summaries = jnp.take(mixed_seq, local_ends, axis=0)
    pool_heads_local = POOL_HEADS // lax.axis_size("tensor")
    pool_width = channels // pool_heads_local
    scale_factor = 1.0 / math.sqrt(pool_width)
    pools_local = pool_query.shape[0]
    queries = pool_query.reshape(pools_local, pool_heads_local, pool_width)
    piece = lax.all_gather(summaries, "seq", axis=0, tiled=True)
    peak = jnp.full((pool_heads_local, pools_local), MASKED, jnp.float32)
    numer = jnp.zeros((pools_local, pool_heads_local, pool_width), jnp.float32)
    count = piece.shape[0]
    seg_index = lax.iota(jnp.int32, count)
    inside = (seg_index[None, :] >= pool_start[:, None]) & (seg_index[None, :] < pool_stop[:, None])
    keys_block = piece.reshape(count, pool_heads_local, pool_width)
    logits = (
        jnp.einsum("pad,rad->apr", queries, keys_block, preferred_element_type=jnp.float32)
        * scale_factor
    )
    logits = jnp.where(inside[None], logits, MASKED)
    new_peak = jnp.maximum(peak, jnp.max(logits, axis=2))
    expo = jnp.where(inside[None], jnp.exp(logits - new_peak[:, :, None]), 0.0)
    rescale = jnp.exp(peak - new_peak)
    denom = jnp.sum(expo, axis=2)
    numer = numer * rescale.T[:, :, None] + jnp.einsum(
        "apr,rad->pad", expo.astype(jnp.bfloat16), keys_block, preferred_element_type=jnp.float32
    )
    peak, denom, numer = (new_peak, denom, numer)
    pooled = (numer / denom.T[:, :, None]).reshape(pools_local, channels)
    return (mixed_seq, pooled)


def solution(mesh):
    in_specs = (
        P(("groups", "seq"), "tensor"),
        P(("groups", "seq"), "tensor"),
        P(("groups", "seq"), None),
        P("tensor", ("groups", "seq")),
        P("tensor", ("groups", "seq")),
        P("tensor"),
        P(None, "tensor"),
        P(),
        P("tensor"),
        P(("groups", "seq")),
        P(("groups", "seq"), "tensor"),
        P(("groups", "seq")),
        P(("groups", "seq")),
    )
    out_specs = (P(("groups", "seq"), "tensor"), P(("groups", "seq"), "tensor"))
    return jax.shard_map(local, mesh=mesh, in_specs=in_specs, out_specs=out_specs, check_vma=False)
```

profile of v0, /device:TPU:0, one launch (start us, length us, event | category | flops | bytes accessed | tf_op | source)
XLA Modules:
  0.0 157.4 jit_solution(5044019205403970520)
XLA Ops:
  7.2 0.0 all-gather.7.cloned.1.call-start
  7.2 0.7 slice.120
  7.9 0.7 slice.121
  8.7 5.0 %collective-permute-start = (bf16[3,1536]{1,0:T(4,128)(2,1)S(1)}, bf16[3,1536]{1,0:T(4,128)(2,1)S(1)}, u32[]{:S(2)}, u32[]{:S(2)}) collective-permute-start(bf16[3,1536]{1,0:T(4,128)(2,1)S(1)} %pad_maximum_fusion.2), channel_id=1, source_target_pairs={{0,4},{4,8},{8,12},{1,5},{5,9},{9,13},{2,6},{6,10},{10,14},{3,7},{... | collective-permute-start | bytes 27656 | tf_op jit(solution)/shard_map/ppermute | solution.py:16
  13.6 0.8 fusion.71
  14.4 0.6 reduce-window.14
  15.0 0.2 slice_reduce_fusion.1
  15.2 0.1 broadcast_add_fusion.1
  15.4 0.6 reduce-window.16
  16.0 0.2 slice_reduce_fusion
  16.2 0.1 broadcast_add_fusion
  16.3 0.8 slice_convert_fusion.3
  17.2 0.8 slice_reduce_fusion.2
  17.9 0.5 fusion.72
  18.5 1.5 fusion.70
  19.9 0.9 convert_reduce_fusion.3
  20.8 0.6 exp.65
  21.5 4.0 %divide_convert_fusion = bf16[512,1280]{1,0:T(8,128)(2,1)S(1)} fusion(bf16[512,1280]{1,0:T(8,128)(2,1)} %param.15, bf16[3,1280]{1,0:T(4,128)(2,1)S(1)} %slice.158, f32[1280]{0:T(1024)S(1)} %get-tuple-element.52, f32[1280]{0:T(1024)S(1)} %get-tuple-element.53, f32[1280]{0:T(1024)S(1)} %get-tuple-element.51, f32[1280]{0:T(1024)S(1)} %get-tuple-element.50), kind=kLoop, calls=%fused_computation.25 | loop fusion | flops 15728640 | bytes 2649600 | tf_op jit(solution)/shard_map/convert_element_type | solution.py:45
  25.5 0.1 fusion.69
  25.6 0.2 copy.34
  25.8 0.2 copy.39
  26.1 1.9 %divide_convert_fusion.1 = bf16[512,256]{1,0:T(8,128)(2,1)S(1)} fusion(bf16[512,256]{1,0:T(8,128)(2,1)} %param.17, bf16[3,256]{1,0:T(4,128)(2,1)S(1)} %slice.165, f32[256]{0:T(256)S(1)} %bitcast.90, f32[256]{0:T(256)S(1)} %bitcast.91, f32[256]{0:T(256)S(1)} %bitcast.89, f32[256]{0:T(256)S(1)} %bitcast.88), kind=kLoop, calls=%fused_computation.59 | loop fusion | flops 3145728 | bytes 529920 | tf_op jit(solution)/shard_map/convert_element_type | solution.py:45
  28.0 1.1 convolution_add_fusion.3
  29.1 1.9 %convolution_add_fusion.2 = f32[20,64,128]{2,1,0:T(8,128)} fusion(bf16[256,20,64]{0,2,1:T(8,128)(2,1)S(1)} %bitcast.75, f32[256,20]{0,1:T(8,128)} %get-tuple-element.72, f32[20,64,128]{2,1,0:T(8,128)S(1)} %convolution_add_fusion.3, f32[20]{0:T(128)} %exp.65, bf16[512,256]{1,0:T(8,128)(2,1)S(1)} %divide_convert_fusion.1), kind=kOutput, calls=%fused_computation.43 | convolution fusion | flops 85196800 | bytes 2052176 | tf_op jit(solution)/shard_map/jhp,js->hps/dot_general | solution.py:61
  31.0 0.0 all-gather.7.cloned.1.call-update
  31.0 0.0 all-gather.5.cloned.1.call-start
  31.1 1.2 dynamic-slice
  33.0 0.9 dynamic-update-slice
  33.8 10.1 %all-reduce = f32[80]{0:T(128)S(1)} all-reduce(f32[80]{0:T(128)S(1)} %dynamic-update-slice), channel_id=2, replica_groups=mesh['groups'=2,'seq'=4,'tensor'=4] {'seq'}, use_global_device_ids=true, to_apply=%add | all-reduce | flops 80 | bytes 640
  44.0 0.1 reshape.210
  44.1 0.7 mul.319
  44.8 0.7 mul.320
  45.4 0.7 compare_and_fusion
  46.2 0.2 fusion.57
  46.3 0.2 fusion.53
  46.5 3.7 %fusion.18 = f32[256,20,64]{0,2,1:T(8,128)} fusion(bf16[256,20,64]{0,2,1:T(8,128)(2,1)S(1)} %bitcast.78, f32[20,256]{1,0:T(8,128)} %get-tuple-element.70, f32[256,256]{1,0:T(8,128)S(1)} %fusion.57, f32[20,256]{1,0:T(8,128)} %bitcast.81, pred[256,256]{1,0:T(8,128)(4,1)S(1)} %iota_compare_fusion), kind=kOutput, calls=%fused_computation.31 | convolution fusion | flops 175636480 | bytes 2334720 | tf_op jit(solution)/shard_map/hij,jhp->ihp/dot_general | solution.py:58
  50.3 2.9 %fusion.17 = f32[256,20,64]{0,2,1:T(8,128)} fusion(bf16[256,20,64]{0,2,1:T(8,128)(2,1)S(1)} %bitcast.76, f32[20,256]{1,0:T(8,128)S(1)} %copy-done.11, f32[256,256]{1,0:T(8,128)S(1)} %fusion.53, f32[20,256]{1,0:T(8,128)S(1)} %bitcast.84, pred[256,256]{1,0:T(8,128)(4,1)S(1)} %iota_compare_fusion), kind=kOutput, calls=%fused_computation.30 | convolution fusion | flops 175636480 | bytes 2334720 | tf_op jit(solution)/shard_map/hij,jhp->ihp/dot_general | solution.py:58
  53.1 33.0 %all-gather.7.cloned.1.call-done = f32[80,64,128]{2,1,0:T(8,128)} async-done(((f32[20,64,128]{2,1,0:T(8,128)}), f32[80,64,128]{2,1,0:T(8,128)}) %all-gather.7.cloned.1.call-update) | async-done | bytes 2621456 | tf_op jit(solution)/shard_map/all_gather | solution.py:21
  86.2 0.1 broadcast.82
  86.3 0.3 fusion.44
  86.6 0.4 copy-done.9
  87.0 0.6 copy-done.3
  87.6 1.4 fusion.21
  89.0 2.8 %copy.40 = f32[256,1280]{1,0:T(8,128)} copy(f32[256,1280]{0,1:T(8,128)} %bitcast.73) | data formatting | bytes 2621440 | tf_op jit(solution)/shard_map/concatenate | solution.py:135
  91.8 0.4 fusion.41
  92.2 0.9 copy-done.2
  93.1 1.4 fusion.22
  94.6 2.9 %copy.41 = f32[256,1280]{1,0:T(8,128)} copy(f32[256,1280]{0,1:T(8,128)} %bitcast.72) | data formatting | bytes 2621440 | tf_op jit(solution)/shard_map/concatenate | solution.py:135
  97.5 4.2 %multiply_reduce_fusion = (f32[512]{0:T(512)S(1)}, f32[512,1280]{1,0:T(8,128)}) fusion(bf16[512,1280]{1,0:T(8,128)(2,1)} %param.16, bf16[512,1280]{1,0:T(8,128)(2,1)S(1)} %divide_convert_fusion, f32[1280]{0:T(1024)S(1)} %copy-done.10, f32[256,1280]{1,0:T(8,128)} %copy.41, f32[256,1280]{1,0:T(8,128)S(1)} %copy-done.1), kind=kLoop, calls=%fused_computation.14 | loop fusion | flops 7208448 | bytes 7871488 | tf_op jit(solution)/shard_map/reduce_sum | solution.py:139
  101.7 6.4 %psum.7 = f32[512]{0:T(512)S(1)} all-reduce(f32[512]{0:T(512)S(1)} %get-tuple-element.66), channel_id=1, replica_groups=mesh['groups'=2,'seq'=4,'tensor'=4] {'tensor'}, use_global_device_ids=true, to_apply=%region_7.8 | all-reduce | flops 512 | bytes 4096 | tf_op jit(solution)/shard_map/psum | solution.py:139
  108.1 2.0 %multiply_convert_fusion.4 = bf16[512,1280]{1,0:T(8,128)(2,1)S(1)} fusion(f32[512,1280]{1,0:T(8,128)} %get-tuple-element.67, f32[1280]{0:T(1024)S(1)} %copy-done.12, f32[512]{0:T(512)S(1)} %add_rsqrt_fusion), kind=kLoop, calls=%fused_computation.13 | loop fusion | flops 1966080 | bytes 3939328 | tf_op jit(solution)/shard_map/convert_element_type | solution.py:143
  110.1 0.0 copy-start
  110.2 0.9 gather_fusion
  111.1 0.8 broadcast_select_fusion
  111.9 0.0 all-gather.5.cloned.1.call-update
  112.0 0.2 reshape.192
  112.2 0.1 fusion.46
  112.3 34.4 %all-gather.5.cloned.1.call-done = bf16[512,1280]{1,0:T(8,128)(2,1)} async-done(((bf16[128,1280]{1,0:T(8,128)(2,1)}), bf16[512,1280]{1,0:T(8,128)(2,1)}) %all-gather.5.cloned.1.call-update) | async-done | bytes 1310736 | tf_op jit(solution)/shard_map/all_gather | solution.py:151
  146.7 1.6 %copy.42 = bf16[512,1280]{0,1:T(8,128)(2,1)S(1)} copy(bf16[512,1280]{1,0:T(8,128)(2,1)} %all-gather.5.cloned.1.call-done) | data formatting | bytes 2621440 | tf_op jit(solution)/shard_map/all_gather | solution.py:151
  148.3 0.4 fusion.73
  148.7 0.3 fusion.31
  149.0 0.6 fusion.28
  149.6 0.1 copy.44
  149.7 0.8 reshape.193
  (52 shorter events, 0.4 us)
Async XLA Ops:
  7.2 79.0 %all-gather.7.cloned.1.call-start = ((), (), s32[]{:S(2)}) async-start(), calls=%async_computation.1 | async-start | bytes 3276800 | tf_op jit(solution)/shard_map/all_gather | solution.py:21
  8.7 12.8 %collective-permute-start = (bf16[3,1536]{1,0:T(4,128)(2,1)S(1)}, bf16[3,1536]{1,0:T(4,128)(2,1)S(1)}, u32[]{:S(2)}, u32[]{:S(2)}) collective-permute-start(bf16[3,1536]{1,0:T(4,128)(2,1)S(1)} %pad_maximum_fusion.2), channel_id=1, source_target_pairs={{0,4},{4,8},{8,12},{1,5},{5,9},{9,13},{2,6},{6,10},{10,14},{3,7},{... | collective-permute-start | bytes 27656 | tf_op jit(solution)/shard_map/ppermute | solution.py:16
  15.3 6.1 %copy-start.4 = (f32[3,8,2,128]{3,1,2,0:T(8,128)}, f32[3,8,2,128]{3,1,2,0:T(8,128)S(1)}, u32[]{:S(2)}) copy-start(f32[3,8,2,128]{3,1,2,0:T(8,128)S(1)} %copy.45) | copy-start | bytes 73732
  16.3 5.1 %copy-start.5 = (f32[3,8,2,128]{3,1,2,0:T(8,128)}, f32[3,8,2,128]{3,1,2,0:T(8,128)S(1)}, u32[]{:S(2)}) copy-start(f32[3,8,2,128]{3,1,2,0:T(8,128)S(1)} %copy.46) | copy-start | bytes 73732
  31.0 115.7 %all-gather.5.cloned.1.call-start = ((), (), s32[]{:S(2)}) async-start(), calls=%async_computation | async-start | bytes 1638400 | tf_op jit(solution)/shard_map/all_gather | solution.py:151
  46.5 3.7 %copy-start.6 = (f32[3,8,2,128]{3,1,2,0:T(8,128)S(1)}, f32[3,8,2,128]{3,1,2,0:T(8,128)}, u32[]{:S(2)}) copy-start(f32[3,8,2,128]{3,1,2,0:T(8,128)} %copy-done.5) | copy-start | bytes 73732
  46.5 3.7 %copy-start.11 = (f32[20,256]{1,0:T(8,128)S(1)}, f32[20,256]{1,0:T(8,128)}, u32[]{:S(2)}) copy-start(f32[20,256]{1,0:T(8,128)} %get-tuple-element.73) | copy-start | bytes 61444
  86.3 0.7 copy-start.9
  86.3 1.3 copy-start.3
  87.6 4.2 %copy-start.13 = (f32[20]{0:T(128)S(1)}, f32[20]{0:T(128)}, u32[]{:S(2)}) copy-start(f32[20]{0:T(128)} %get-tuple-element.84) | copy-start | bytes 244
  89.0 3.2 %copy-start.8 = (f32[256,20]{0,1:T(8,128)S(1)}, f32[256,20]{0,1:T(8,128)}, u32[]{:S(2)}) copy-start(f32[256,20]{0,1:T(8,128)} %get-tuple-element.76) | copy-start | bytes 61444
  91.8 1.3 copy-start.2
  94.6 2.9 %copy-start.1 = (f32[256,1280]{1,0:T(8,128)S(1)}, f32[256,1280]{1,0:T(8,128)}, u32[]{:S(2)}) copy-start(f32[256,1280]{1,0:T(8,128)} %copy.40) | copy-start | bytes 3932164
  94.6 2.9 %copy-start.10 = (f32[1280]{0:T(1024)S(1)}, f32[1280]{0:T(1024)}, u32[]{:S(2)}) copy-start(f32[1280]{0:T(1024)} %mul.320) | copy-start | bytes 15364
  97.5 10.6 %copy-start.12 = (f32[1280]{0:T(1024)S(1)}, f32[1280]{0:T(1024)}, u32[]{:S(2)}) copy-start(f32[1280]{0:T(1024)} %param.23) | copy-start | bytes 15364
  110.1 38.2 %copy-start = (bf16[512,1280]{1,0:T(8,128)(2,1)}, bf16[512,1280]{1,0:T(8,128)(2,1)S(1)}, u32[]{:S(2)}) copy-start(bf16[512,1280]{1,0:T(8,128)(2,1)S(1)} %multiply_convert_fusion.4) | copy-start | bytes 3932164
  110.2 1.8 %copy-start.7 = (bf16[40,1280]{1,0:T(8,128)(2,1)S(1)}, bf16[40,1280]{1,0:T(8,128)(2,1)}, u32[]{:S(2)}) copy-start(bf16[40,1280]{1,0:T(8,128)(2,1)} %param.25) | copy-start | bytes 307204
  110.2 2.0 %copy-start.14 = (s32[40]{0:T(128)S(1)}, s32[40]{0:T(128)}, u32[]{:S(2)}) copy-start(s32[40]{0:T(128)} %param.27) | copy-start | bytes 484
  110.2 2.0 %copy-start.15 = (s32[40]{0:T(128)S(1)}, s32[40]{0:T(128)}, u32[]{:S(2)}) copy-start(s32[40]{0:T(128)} %param.26) | copy-start | bytes 484
Sparse Core Ops, SparseCore 0:
  31.1 55.0 all-gather.6
  112.1 34.5 all-gather.4
where the time goes:
time: 158 us; the launch traced here: 157 us
  waiting for transfers between devices  67.5 us (43%)
  other arithmetic  20 us (13%)
  local copies, waits for them, and re-layouts  18.7 us (12%)
  blocking collectives  16.5 us (10%)
  between operations  15.1 us (10%)
  matrix products  14.5 us (9%)
  starting transfers between devices  5.04 us (3%)
    all_gather x1, waiting for transfers between devices, local(): piece = lax.all_gather(summaries, 'seq', axis=0, tiled=True)  34.4 us
    all_gather x1, waiting for transfers between devices, prefix(): gathered = jax.tree.map(lambda a: lax.all_gather(a, axis), part)  33 us
    unnamed x1, blocking collectives  10.1 us
    dot_general x2, matrix products, stretch_local(): jnp.einsum('hij,jhp->ihp', mixing, x_block, preferred_element_type=jnp.fl...  6.59 us
    psum x1, blocking collectives, local(): square_sum = lax.psum(jnp.sum(gated * gated, axis=1), 'tensor')  6.37 us
    convert_element_type x2, other arithmetic, causal_conv(): return silu_act(summed).astype(jnp.bfloat16)  5.91 us
    concatenate x2, local copies, waits for them, and re-layouts, local(): jnp.concatenate(pieces_out, axis=0)  5.7 us
    ppermute x1, starting transfers between devices, passed_along(): lax.ppermute(value, axis, [(source, source + steps) for source in range(l...  4.96 us
  transfers between devices with their start and end apart: 3, of which 2 were waited for; matrix products, arithmetic and copies ran while one was open for 12% of the time, Pallas kernels for 0%

commit v1 on v0

--- a/solution.py
+++ b/solution.py
@@ -136,7 +136,7 @@
         jnp.float32
     )
     gated = ssd_out.reshape(tok_rows, channels) * silu_act(z_gate.astype(jnp.float32))
-    square_sum = lax.psum(jnp.sum(gated * gated, axis=1), "tensor")
+    square_sum = jnp.sum(lax.all_gather(jnp.sum(gated * gated, axis=1), "tensor"), axis=0)
     width_all = channels * lax.axis_size("tensor")
     mixed_seq = (
         gated * lax.rsqrt(square_sum / width_all + EPSILON)[:, None] * norm_gain[None, :]

time: 158 us -> 158 us (level)
    psum x1 -> x0, blocking collectives: 6.37 us -> none  [local(): square_sum = lax.psum(jnp.sum(gated * gated, axis=1), 'tensor')]
    all_gather x0 -> x1, blocking collectives: none -> 5.18 us  [local(): lax.all_gather(jnp.sum(gated * gated, axis=1), 'tensor')]
    reduce_sum x1 -> x2, other arithmetic: 4.24 us -> 4.27 us  [the longest x1 4.24 us: local(): jnp.sum(gated * gated, axis=1)]
where the time goes in v1:
time: 158 us; the launch traced here: 157 us
  waiting for transfers between devices  67.9 us (43%)
  other arithmetic  20.1 us (13%)
  local copies, waits for them, and re-layouts  18.7 us (12%)
  blocking collectives  15.3 us (10%)
  between operations  15.1 us (10%)
  matrix products  14.5 us (9%)
  starting transfers between devices  5.04 us (3%)
    all_gather x1, waiting for transfers between devices, local(): piece = lax.all_gather(summaries, 'seq', axis=0, tiled=True)  34.9 us
    all_gather x1, waiting for transfers between devices, prefix(): gathered = jax.tree.map(lambda a: lax.all_gather(a, axis), part)  33 us
    unnamed x1, blocking collectives  10.1 us
    dot_general x2, matrix products, stretch_local(): jnp.einsum('hij,jhp->ihp', mixing, x_block, preferred_element_type=jnp.fl...  6.59 us
    convert_element_type x2, other arithmetic, causal_conv(): return silu_act(summed).astype(jnp.bfloat16)  5.91 us
    concatenate x2, local copies, waits for them, and re-layouts, local(): jnp.concatenate(pieces_out, axis=0)  5.7 us
    all_gather x1, blocking collectives, local(): lax.all_gather(jnp.sum(gated * gated, axis=1), 'tensor')  5.18 us
    ppermute x1, starting transfers between devices, passed_along(): lax.ppermute(value, axis, [(source, source + steps) for source in range(l...  4.96 us
  transfers between devices with their start and end apart: 3, of which 2 were waited for; matrix products, arithmetic and copies ran while one was open for 12% of the time, Pallas kernels for 0%

profile of v1, /device:TPU:0, one launch (start us, length us, event | category | flops | bytes accessed | tf_op | source)
XLA Modules:
  0.0 156.7 jit_solution(1446903970156979110)
XLA Ops:
  7.2 0.0 all-gather.9.cloned.1.call-start
  7.2 0.7 slice.120
  7.9 0.7 slice.121
  8.7 5.0 %collective-permute-start = (bf16[3,1536]{1,0:T(4,128)(2,1)S(1)}, bf16[3,1536]{1,0:T(4,128)(2,1)S(1)}, u32[]{:S(2)}, u32[]{:S(2)}) collective-permute-start(bf16[3,1536]{1,0:T(4,128)(2,1)S(1)} %pad_maximum_fusion.2), channel_id=1, source_target_pairs={{0,4},{4,8},{8,12},{1,5},{5,9},{9,13},{2,6},{6,10},{10,14},{3,7},{... | collective-permute-start | bytes 27656 | tf_op jit(solution)/shard_map/ppermute | solution.py:16
  13.6 0.8 fusion.71
  14.4 0.6 reduce-window.14
  15.0 0.2 slice_reduce_fusion.1
  15.2 0.1 broadcast_add_fusion.1
  15.4 0.6 reduce-window.16
  16.0 0.2 slice_reduce_fusion
  16.2 0.1 broadcast_add_fusion
  16.3 0.8 slice_convert_fusion.3
  17.2 0.8 slice_reduce_fusion.2
  17.9 0.5 fusion.72
  18.5 1.5 fusion.70
  19.9 0.9 convert_reduce_fusion.3
  20.8 0.6 exp.65
  21.5 4.0 %divide_convert_fusion = bf16[512,1280]{1,0:T(8,128)(2,1)S(1)} fusion(bf16[512,1280]{1,0:T(8,128)(2,1)} %param.15, bf16[3,1280]{1,0:T(4,128)(2,1)S(1)} %slice.158, f32[1280]{0:T(1024)S(1)} %get-tuple-element.52, f32[1280]{0:T(1024)S(1)} %get-tuple-element.53, f32[1280]{0:T(1024)S(1)} %get-tuple-element.51, f32[1280]{0:T(1024)S(1)} %get-tuple-element.50), kind=kLoop, calls=%fused_computation.25 | loop fusion | flops 15728640 | bytes 2649600 | tf_op jit(solution)/shard_map/convert_element_type | solution.py:45
  25.5 0.1 fusion.69
  25.6 0.2 copy.34
  25.8 0.2 copy.39
  26.1 1.9 %divide_convert_fusion.1 = bf16[512,256]{1,0:T(8,128)(2,1)S(1)} fusion(bf16[512,256]{1,0:T(8,128)(2,1)} %param.17, bf16[3,256]{1,0:T(4,128)(2,1)S(1)} %slice.165, f32[256]{0:T(256)S(1)} %bitcast.92, f32[256]{0:T(256)S(1)} %bitcast.93, f32[256]{0:T(256)S(1)} %bitcast.91, f32[256]{0:T(256)S(1)} %bitcast.90), kind=kLoop, calls=%fused_computation.59 | loop fusion | flops 3145728 | bytes 529920 | tf_op jit(solution)/shard_map/convert_element_type | solution.py:45
  28.0 1.1 convolution_add_fusion.3
  29.1 1.9 %convolution_add_fusion.2 = f32[20,64,128]{2,1,0:T(8,128)} fusion(bf16[256,20,64]{0,2,1:T(8,128)(2,1)S(1)} %bitcast.76, f32[256,20]{0,1:T(8,128)} %get-tuple-element.72, f32[20,64,128]{2,1,0:T(8,128)S(1)} %convolution_add_fusion.3, f32[20]{0:T(128)} %exp.65, bf16[512,256]{1,0:T(8,128)(2,1)S(1)} %divide_convert_fusion.1), kind=kOutput, calls=%fused_computation.43 | convolution fusion | flops 85196800 | bytes 2052176 | tf_op jit(solution)/shard_map/jhp,js->hps/dot_general | solution.py:61
  31.0 0.0 all-gather.9.cloned.1.call-update
  31.0 0.0 all-gather.7.cloned.1.call-start
  31.1 1.2 dynamic-slice
  33.0 0.9 dynamic-update-slice
  33.8 10.1 %all-reduce = f32[80]{0:T(128)S(1)} all-reduce(f32[80]{0:T(128)S(1)} %dynamic-update-slice), channel_id=2, replica_groups=mesh['groups'=2,'seq'=4,'tensor'=4] {'seq'}, use_global_device_ids=true, to_apply=%add | all-reduce | flops 80 | bytes 640
  44.0 0.1 reshape.214
  44.1 0.7 mul.319
  44.8 0.7 mul.320
  45.4 0.7 compare_and_fusion
  46.2 0.2 fusion.57
  46.3 0.2 fusion.53
  46.5 3.7 %fusion.18 = f32[256,20,64]{0,2,1:T(8,128)} fusion(bf16[256,20,64]{0,2,1:T(8,128)(2,1)S(1)} %bitcast.79, f32[20,256]{1,0:T(8,128)} %get-tuple-element.70, f32[256,256]{1,0:T(8,128)S(1)} %fusion.57, f32[20,256]{1,0:T(8,128)} %bitcast.82, pred[256,256]{1,0:T(8,128)(4,1)S(1)} %iota_compare_fusion), kind=kOutput, calls=%fused_computation.31 | convolution fusion | flops 175636480 | bytes 2334720 | tf_op jit(solution)/shard_map/hij,jhp->ihp/dot_general | solution.py:58
  50.3 2.9 %fusion.17 = f32[256,20,64]{0,2,1:T(8,128)} fusion(bf16[256,20,64]{0,2,1:T(8,128)(2,1)S(1)} %bitcast.77, f32[20,256]{1,0:T(8,128)S(1)} %copy-done.11, f32[256,256]{1,0:T(8,128)S(1)} %fusion.53, f32[20,256]{1,0:T(8,128)S(1)} %bitcast.85, pred[256,256]{1,0:T(8,128)(4,1)S(1)} %iota_compare_fusion), kind=kOutput, calls=%fused_computation.30 | convolution fusion | flops 175636480 | bytes 2334720 | tf_op jit(solution)/shard_map/hij,jhp->ihp/dot_general | solution.py:58
  53.1 33.0 %all-gather.9.cloned.1.call-done = f32[80,64,128]{2,1,0:T(8,128)} async-done(((f32[20,64,128]{2,1,0:T(8,128)}), f32[80,64,128]{2,1,0:T(8,128)}) %all-gather.9.cloned.1.call-update) | async-done | bytes 2621456 | tf_op jit(solution)/shard_map/all_gather | solution.py:21
  86.2 0.1 broadcast.89
  86.3 0.3 fusion.44
  86.6 0.4 copy-done.9
  87.0 0.6 copy-done.3
  87.6 1.4 fusion.21
  89.0 2.8 %copy.40 = f32[256,1280]{1,0:T(8,128)} copy(f32[256,1280]{0,1:T(8,128)} %bitcast.74) | data formatting | bytes 2621440 | tf_op jit(solution)/shard_map/concatenate | solution.py:135
  91.8 0.4 fusion.41
  92.2 0.9 copy-done.2
  93.1 1.4 fusion.22
  94.6 2.9 %copy.41 = f32[256,1280]{1,0:T(8,128)} copy(f32[256,1280]{0,1:T(8,128)} %bitcast.73) | data formatting | bytes 2621440 | tf_op jit(solution)/shard_map/concatenate | solution.py:135
  97.5 4.2 %multiply_reduce_fusion = (f32[512]{0:T(512)S(1)}, f32[512,1280]{1,0:T(8,128)}) fusion(bf16[512,1280]{1,0:T(8,128)(2,1)} %param.16, bf16[512,1280]{1,0:T(8,128)(2,1)S(1)} %divide_convert_fusion, f32[1280]{0:T(1024)S(1)} %copy-done.10, f32[256,1280]{1,0:T(8,128)} %copy.41, f32[256,1280]{1,0:T(8,128)S(1)} %copy-done.1), kind=kLoop, calls=%fused_computation.14 | loop fusion | flops 7208448 | bytes 7871488 | tf_op jit(solution)/shard_map/reduce_sum | solution.py:139
  101.7 5.2 %all-gather.3 = f32[4,1,512]{2,1,0:T(1,128)S(1)} all-gather(f32[1,1,512]{2,1,0:T(1,128)S(1)} %bitcast.88), channel_id=4, replica_groups=mesh['groups'=2,'seq'=4,'tensor'=4] {'tensor'}, dimensions={0}, use_global_device_ids=true | all-gather | bytes 10240 | tf_op jit(solution)/shard_map/all_gather | solution.py:139
  107.0 2.0 %multiply_convert_fusion.4 = bf16[512,1280]{1,0:T(8,128)(2,1)S(1)} fusion(f32[512,1280]{1,0:T(8,128)} %get-tuple-element.67, f32[1280]{0:T(1024)S(1)} %copy-done.12, f32[512]{0:T(512)S(1)} %add_rsqrt_fusion), kind=kLoop, calls=%fused_computation.13 | loop fusion | flops 1966080 | bytes 3939328 | tf_op jit(solution)/shard_map/convert_element_type | solution.py:143
  109.0 0.0 copy-start.14
  109.0 0.9 gather_fusion
  109.9 0.8 broadcast_select_fusion
  110.8 0.0 all-gather.7.cloned.1.call-update
  110.8 0.2 reshape.196
  111.0 0.1 fusion.46
  111.1 34.9 %all-gather.7.cloned.1.call-done = bf16[512,1280]{1,0:T(8,128)(2,1)} async-done(((bf16[128,1280]{1,0:T(8,128)(2,1)}), bf16[512,1280]{1,0:T(8,128)(2,1)}) %all-gather.7.cloned.1.call-update) | async-done | bytes 1310736 | tf_op jit(solution)/shard_map/all_gather | solution.py:151
  146.0 1.6 %copy.42 = bf16[512,1280]{0,1:T(8,128)(2,1)S(1)} copy(bf16[512,1280]{1,0:T(8,128)(2,1)} %all-gather.7.cloned.1.call-done) | data formatting | bytes 2621440 | tf_op jit(solution)/shard_map/all_gather | solution.py:151
  147.6 0.4 fusion.73
  148.0 0.3 fusion.31
  148.3 0.6 fusion.28
  148.9 0.1 copy.44
  149.0 0.8 reshape.197
  (53 shorter events, 0.4 us)
Async XLA Ops:
  7.2 79.0 %all-gather.9.cloned.1.call-start = ((), (), s32[]{:S(2)}) async-start(), calls=%async_computation.1 | async-start | bytes 3276800 | tf_op jit(solution)/shard_map/all_gather | solution.py:21
  8.7 12.8 %collective-permute-start = (bf16[3,1536]{1,0:T(4,128)(2,1)S(1)}, bf16[3,1536]{1,0:T(4,128)(2,1)S(1)}, u32[]{:S(2)}, u32[]{:S(2)}) collective-permute-start(bf16[3,1536]{1,0:T(4,128)(2,1)S(1)} %pad_maximum_fusion.2), channel_id=1, source_target_pairs={{0,4},{4,8},{8,12},{1,5},{5,9},{9,13},{2,6},{6,10},{10,14},{3,7},{... | collective-permute-start | bytes 27656 | tf_op jit(solution)/shard_map/ppermute | solution.py:16
  15.3 6.1 %copy-start.4 = (f32[3,8,2,128]{3,1,2,0:T(8,128)}, f32[3,8,2,128]{3,1,2,0:T(8,128)S(1)}, u32[]{:S(2)}) copy-start(f32[3,8,2,128]{3,1,2,0:T(8,128)S(1)} %copy.45) | copy-start | bytes 73732
  16.3 5.1 %copy-start.5 = (f32[3,8,2,128]{3,1,2,0:T(8,128)}, f32[3,8,2,128]{3,1,2,0:T(8,128)S(1)}, u32[]{:S(2)}) copy-start(f32[3,8,2,128]{3,1,2,0:T(8,128)S(1)} %copy.46) | copy-start | bytes 73732
  31.0 115.0 %all-gather.7.cloned.1.call-start = ((), (), s32[]{:S(2)}) async-start(), calls=%async_computation | async-start | bytes 1638400 | tf_op jit(solution)/shard_map/all_gather | solution.py:151
  46.5 3.7 %copy-start.6 = (f32[3,8,2,128]{3,1,2,0:T(8,128)S(1)}, f32[3,8,2,128]{3,1,2,0:T(8,128)}, u32[]{:S(2)}) copy-start(f32[3,8,2,128]{3,1,2,0:T(8,128)} %copy-done.5) | copy-start | bytes 73732
  46.5 3.7 %copy-start.11 = (f32[20,256]{1,0:T(8,128)S(1)}, f32[20,256]{1,0:T(8,128)}, u32[]{:S(2)}) copy-start(f32[20,256]{1,0:T(8,128)} %get-tuple-element.73) | copy-start | bytes 61444
  86.3 0.7 copy-start.9
  86.3 1.3 copy-start.3
  87.6 4.2 %copy-start.13 = (f32[20]{0:T(128)S(1)}, f32[20]{0:T(128)}, u32[]{:S(2)}) copy-start(f32[20]{0:T(128)} %get-tuple-element.84) | copy-start | bytes 244
  89.0 3.2 %copy-start.8 = (f32[256,20]{0,1:T(8,128)S(1)}, f32[256,20]{0,1:T(8,128)}, u32[]{:S(2)}) copy-start(f32[256,20]{0,1:T(8,128)} %get-tuple-element.76) | copy-start | bytes 61444
  91.8 1.3 copy-start.2
  94.6 2.9 %copy-start.1 = (f32[256,1280]{1,0:T(8,128)S(1)}, f32[256,1280]{1,0:T(8,128)}, u32[]{:S(2)}) copy-start(f32[256,1280]{1,0:T(8,128)} %copy.40) | copy-start | bytes 3932164
  94.6 2.9 %copy-start.10 = (f32[1280]{0:T(1024)S(1)}, f32[1280]{0:T(1024)}, u32[]{:S(2)}) copy-start(f32[1280]{0:T(1024)} %mul.320) | copy-start | bytes 15364
  97.5 9.5 %copy-start.12 = (f32[1280]{0:T(1024)S(1)}, f32[1280]{0:T(1024)}, u32[]{:S(2)}) copy-start(f32[1280]{0:T(1024)} %param.23) | copy-start | bytes 15364
  109.0 38.6 %copy-start = (bf16[512,1280]{1,0:T(8,128)(2,1)}, bf16[512,1280]{1,0:T(8,128)(2,1)S(1)}, u32[]{:S(2)}) copy-start(bf16[512,1280]{1,0:T(8,128)(2,1)S(1)} %multiply_convert_fusion.4) | copy-start | bytes 3932164
  109.0 1.8 %copy-start.7 = (bf16[40,1280]{1,0:T(8,128)(2,1)S(1)}, bf16[40,1280]{1,0:T(8,128)(2,1)}, u32[]{:S(2)}) copy-start(bf16[40,1280]{1,0:T(8,128)(2,1)} %param.25) | copy-start | bytes 307204
  109.0 2.0 %copy-start.14 = (s32[40]{0:T(128)S(1)}, s32[40]{0:T(128)}, u32[]{:S(2)}) copy-start(s32[40]{0:T(128)} %param.27) | copy-start | bytes 484
  109.0 2.0 %copy-start.15 = (s32[40]{0:T(128)S(1)}, s32[40]{0:T(128)}, u32[]{:S(2)}) copy-start(s32[40]{0:T(128)} %param.26) | copy-start | bytes 484
Sparse Core Ops, SparseCore 0:
  31.1 55.0 all-gather.8
  110.9 35.0 all-gather.6
